TPU v7x, 512 devices: a whole 4x8x8 slice. The times are simulated.
512 devices in a mesh: dp: 8 (over z), cent: 64 (over x, y, core).
Axes of the slice: x: 4, y: 8, z: 8, core: 2. Of those that a mesh axis runs over, the one named last changes fastest.
Arguments:
- points: bfloat16 [24576, 1024], P(('dp', 'cent')), may hold values from -6 to 6
- assign: int32 [24576], P(('dp', 'cent')), may hold values from 0 to 32767, as said below
- centroids: float32 [32768, 1024], P('cent'), may hold values from -6 to 6
- counts: int32 [32768], P('cent'), may hold values from 1 to 4
Outputs:
- new_centroids: float32 [32768, 1024], P('cent')
- best: float32 [24576], P(('dp', 'cent'))
Inputs may be any that keep to these rules, and one draw needn't show every extreme that they name: `assign`: split the points into aligned blocks of 3072 points in order (the points of one dp index). In every block, the clusters k * 512 to (k + 1) * 512 - 1 receive exactly 48 points together, for every k.
All inputs are finite; a program needn't handle non-finite values.
Results may differ from a plain program's by a relative error of at most 0.0003.
Values may be sent and summed in bfloat16 or wider, within the bound.
No kernel may reach another device: no remote copies, remote signals or barrier semaphores. Data moves between devices by JAX's collectives and lax.ppermute only.
A program may use at most 128 MiB of HBM per device.

v0:
```python
import jax
import jax.numpy as jnp
from jax import lax
from jax.sharding import PartitionSpec as P


def renorm(merged):
    return merged * lax.rsqrt(jnp.mean(merged * merged, axis=1, keepdims=True) + 1e-05)


def cluster_terms(rows, labels, kdev):
    first = lax.axis_index("cent") * kdev
    local = labels - first
    onehot = (local[None, :] == jnp.arange(kdev, dtype=jnp.int32)[:, None]).astype(jnp.bfloat16)
    return jnp.dot(onehot, rows, preferred_element_type=jnp.float32)


def per_device(points, assign, centroids, counts):
    kdev = centroids.shape[0]
    pdev = points.shape[0]
    weighted = centroids * counts.astype(jnp.float32)[:, None]
    rows, labels = (
        lax.all_gather(points, "cent", axis=0, tiled=True),
        lax.all_gather(assign, "cent", axis=0, tiled=True),
    )
    sums = cluster_terms(rows, labels, kdev)
    total = lax.psum(sums, "dp")
    fresh = renorm(weighted + total)
    rounded = fresh.astype(jnp.bfloat16)
    scores = jnp.dot(rows, rounded.T, preferred_element_type=jnp.float32)
    local_best = jnp.max(scores, axis=1)
    merged_best = lax.pmax(local_best, "cent")
    top = lax.dynamic_slice_in_dim(merged_best, lax.axis_index("cent") * pdev, pdev, 0)
    values = points.astype(jnp.float32)
    width = points.shape[1]
    scale = width * jnp.sqrt(jnp.mean(values * values, axis=1) + 1e-06)
    return (fresh, top / scale)


def solution(mesh):
    placed = (P(("dp", "cent"), None), P(("dp", "cent")), P("cent", None), P("cent"))
    return jax.shard_map(
        per_device,
        mesh=mesh,
        in_specs=placed,
        out_specs=(P("cent", None), P(("dp", "cent"))),
        check_vma=False,
    )
```

profile of v0, /device:TPU:64, one launch (start us, length us, event | category | flops | bytes accessed | tf_op | source)
XLA Modules:
  0.0 617.8 jit_solution(2940238520247544569)
XLA Ops:
  7.2 0.0 all-gather.2.cloned.1.call-start
  7.2 0.7 all-gather.2.cloned.1.call-update
  7.9 0.0 all-reduce.3.cloned.1.call-start
  7.9 1.3 dynamic-slice
  9.9 0.9 dynamic-update-slice
  10.8 251.6 %all-reduce = s32[3072]{0:T(1024)S(1)} all-reduce(s32[3072]{0:T(1024)S(1)} %dynamic-update-slice), channel_id=1, replica_groups=mesh['dp'=8,'cent'=64] {'cent'}, use_global_device_ids=true, to_apply=%add | all-reduce | flops 3072 | bytes 24576
  262.4 0.0 all-gather.2.cloned.1.call-done
  262.4 0.0 copy-start.3
  262.4 7.5 %fusion = f32[512,1024]{1,0:T(8,128)} fusion(bf16[3072,1024]{1,0:T(8,128)(2,1)} %all-gather.2.cloned.1.call-done, s32[3072]{0:T(1024)S(1)} %broadcast_subtract_fusion), kind=kOutput, calls=%fused_computation.1 | convolution fusion | flops 3222798336 | bytes 8400896 | tf_op jit(solution)/shard_map/dot_general | solution.py:15
  269.9 0.0 copy-start.4
  269.9 0.0 copy-start
  269.9 0.0 all-reduce.3.cloned.1.call-update
  269.9 0.7 copy-done.4
  270.6 0.0 copy-done.3
  270.6 0.1 multiply_reduce_fusion.1
  270.7 83.2 %all-reduce.3.cloned.1.call-done = f32[512,1024]{1,0:T(8,128)} async-done(((f32[512,1024]{1,0:T(8,128)}), f32[512,1024]{1,0:T(8,128)}) %all-reduce.3.cloned.1.call-update) | async-done | bytes 2097168 | tf_op jit(solution)/shard_map/psum | solution.py:27
  353.9 0.0 copy-done
  353.9 0.0 copy-start.1
  353.9 2.2 multiply_reduce_fusion
  356.1 0.1 copy-done.1
  356.1 0.0 copy-start.5
  356.1 0.4 broadcast_multiply_fusion
  356.5 0.0 copy-start.2
  356.5 1.3 copy-done.2
  357.8 1.8 copy-done.5
  359.7 3.7 convolution_reduce_fusion
  363.4 247.0 %pmax.7 = f32[3072]{0:T(1024)S(1)} all-reduce(f32[3072]{0:T(1024)S(1)} %convolution_reduce_fusion), channel_id=1, replica_groups=mesh['dp'=8,'cent'=64] {'cent'}, use_global_device_ids=true, to_apply=%region_3.0 | all-reduce | flops 3072 | bytes 24576 | tf_op jit(solution)/shard_map/pmax | solution.py:32
  610.4 0.6 multiply_divide_fusion
  (4 shorter events, 0.0 us)
Async XLA Ops:
  7.2 255.2 %all-gather.2.cloned.1.call-start = ((), (), s32[]{:S(2)}) async-start(), calls=%async_computation | async-start | bytes 6389760 | tf_op jit(solution)/shard_map/all_gather | solution.py:23
  7.9 346.0 %all-reduce.3.cloned.1.call-start = ((), (), s32[]{:S(2)}) async-start(), calls=%async_computation.1 | async-start | bytes 4194304 | tf_op jit(solution)/shard_map/psum | solution.py:27
  262.4 8.2 %copy-start.3 = (bf16[48,1024]{1,0:T(8,128)(2,1)S(1)}, bf16[48,1024]{1,0:T(8,128)(2,1)}, u32[]{:S(2)}) copy-start(bf16[48,1024]{1,0:T(8,128)(2,1)} %param.4) | copy-start | bytes 294916
  269.9 0.7 copy-start.4
  269.9 84.0 %copy-start = (f32[512,1024]{1,0:T(8,128)S(1)}, f32[512,1024]{1,0:T(8,128)}, u32[]{:S(2)}) copy-start(f32[512,1024]{1,0:T(8,128)} %param.6) | copy-start | bytes 6291460
  353.9 2.2 copy-start.1
  356.1 3.5 copy-start.5
  356.5 1.3 copy-start.2
Sparse Core Ops, SparseCore 0:
  11.3 89.7 all-gather.1
  270.1 83.7 all-reduce.2
where the time goes:
time: 618 us
  blocking collectives  499 us (81%)
  waiting for transfers between devices  83.9 us (14%)
  between operations  14.7 us (2%)
  matrix products  11.3 us (2%)
    unnamed x1, blocking collectives  252 us
    pmax x1, blocking collectives, per_device(): merged_best = lax.pmax(local_best, 'cent')  247 us
    psum x1, waiting for transfers between devices, per_device(): total = lax.psum(sums, 'dp')  83.2 us
  transfers between devices with their start and end apart: 2, of which 1 were waited for; matrix products, arithmetic and copies ran while one was open for 0% of the time, Pallas kernels for 0%

commit v1 on v0

--- a/solution.py
+++ b/solution.py
@@ -24,7 +24,10 @@
         lax.all_gather(assign, "cent", axis=0, tiled=True),
     )
     sums = cluster_terms(rows, labels, kdev)
-    total = lax.psum(sums, "dp")
+    count, total = (lax.axis_size("dp"), sums)
+    for far in [1 << k for k in range(count.bit_length() - 1)]:
+        swap = [(i, i ^ far) for i in range(count)]
+        total = total + lax.ppermute(total, "dp", swap)
     fresh = renorm(weighted + total)
     rounded = fresh.astype(jnp.bfloat16)
     scores = jnp.dot(rows, rounded.T, preferred_element_type=jnp.float32)

time: 618 us -> 773 us (1.25)
  the two profiles are of different devices: /device:TPU:64 before, /device:TPU:192 now
where the time goes in v1:
time: 773 us; the launch traced here: 772 us
  blocking collectives  505 us (65%)
  waiting for transfers between devices  221 us (29%)
  between operations  14.8 us (2%)
  matrix products  12.7 us (2%)
  starting transfers between devices  12.2 us (2%)
    pmax x1, blocking collectives, per_device(): merged_best = lax.pmax(local_best, 'cent')  253 us
    unnamed x1, blocking collectives  252 us
    ppermute x3, waiting for transfers between devices, per_device(): total = total + lax.ppermute(total, 'dp', swap)  221 us
  transfers between devices with their start and end apart: 4, of which 3 were waited for; matrix products, arithmetic and copies ran while one was open for 0% of the time, Pallas kernels for 0%

profile of v1, /device:TPU:192, one launch (start us, length us, event | category | flops | bytes accessed | tf_op | source)
XLA Modules:
  0.0 772.2 jit_solution(5320542348832728749)
XLA Ops:
  7.2 0.0 all-gather.2.cloned.1.call-start
  7.2 0.7 all-gather.2.cloned.1.call-update
  7.9 1.3 dynamic-slice
  9.8 0.9 dynamic-update-slice
  10.7 251.6 %all-reduce = s32[3072]{0:T(1024)S(1)} all-reduce(s32[3072]{0:T(1024)S(1)} %dynamic-update-slice), channel_id=1, replica_groups=mesh['dp'=8,'cent'=64] {'cent'}, use_global_device_ids=true, to_apply=%add | all-reduce | flops 3072 | bytes 24576
  262.3 0.0 all-gather.2.cloned.1.call-done
  262.3 5.5 fusion
  267.8 1.9 collective-permute-start
  269.7 42.4 %collective-permute-done = f32[512,1024]{1,0:T(8,128)S(1)} collective-permute-done((f32[512,1024]{1,0:T(8,128)S(1)}, f32[512,1024]{1,0:T(8,128)S(1)}, u32[]{:S(2)}, u32[]{:S(2)}) %collective-permute-start) | collective-permute-done | bytes 2097184 | tf_op jit(solution)/shard_map/ppermute | solution.py:30
  312.1 0.4 add.32
  312.5 0.0 copy-start.2
  312.5 0.0 copy-start.1
  312.5 2.1 collective-permute-start.1
  314.6 87.3 %collective-permute-done.1 = f32[512,1024]{1,0:T(8,128)S(1)} collective-permute-done((f32[512,1024]{1,0:T(8,128)S(1)}, f32[512,1024]{1,0:T(8,128)S(1)}, u32[]{:S(2)}, u32[]{:S(2)}) %collective-permute-start.1) | collective-permute-done | bytes 2097184 | tf_op jit(solution)/shard_map/ppermute | solution.py:30
  401.9 0.4 add.33
  402.3 8.2 %collective-permute-start.2 = (f32[512,1024]{1,0:T(8,128)S(1)}, f32[512,1024]{1,0:T(8,128)}, u32[]{:S(2)}, u32[]{:S(2)}) collective-permute-start(f32[512,1024]{1,0:T(8,128)S(1)} %add.33), channel_id=1, source_target_pairs={{0,256},{64,320},{128,384},{192,448},{256,0},{320,64},{384,128},{4... | collective-permute-start | bytes 6291464 | tf_op jit(solution)/shard_map/ppermute | solution.py:30
  410.5 0.0 copy-done.2
  410.5 0.0 copy-done.1
  410.5 0.1 multiply_reduce_fusion.1
  410.6 90.8 %collective-permute-done.2 = f32[512,1024]{1,0:T(8,128)} collective-permute-done((f32[512,1024]{1,0:T(8,128)S(1)}, f32[512,1024]{1,0:T(8,128)}, u32[]{:S(2)}, u32[]{:S(2)}) %collective-permute-start.2) | collective-permute-done | bytes 2097184 | tf_op jit(solution)/shard_map/ppermute | solution.py:30
  501.5 2.7 multiply_reduce_fusion
  504.2 0.2 broadcast_multiply_fusion
  504.4 0.0 copy-start
  504.4 7.2 convolution_reduce_fusion
  511.7 0.0 copy-done
  511.7 253.0 %pmax.7 = f32[3072]{0:T(1024)S(1)} all-reduce(f32[3072]{0:T(1024)S(1)} %convolution_reduce_fusion), channel_id=1, replica_groups=mesh['dp'=8,'cent'=64] {'cent'}, use_global_device_ids=true, to_apply=%region_2.0 | all-reduce | flops 3072 | bytes 24576 | tf_op jit(solution)/shard_map/pmax | solution.py:35
  764.7 0.6 multiply_divide_fusion
  (4 shorter events, 0.0 us)
Async XLA Ops:
  7.2 255.1 %all-gather.2.cloned.1.call-start = ((), (), s32[]{:S(2)}) async-start(), calls=%async_computation | async-start | bytes 6389760 | tf_op jit(solution)/shard_map/all_gather | solution.py:23
  267.8 44.3 %collective-permute-start = (f32[512,1024]{1,0:T(8,128)S(1)}, f32[512,1024]{1,0:T(8,128)S(1)}, u32[]{:S(2)}, u32[]{:S(2)}) collective-permute-start(f32[512,1024]{1,0:T(8,128)S(1)} %fusion), channel_id=1, source_target_pairs={{0,64},{64,0},{128,192},{192,128},{256,320},{320,256},{384,448},{4... | collective-permute-start | bytes 6291464 | tf_op jit(solution)/shard_map/ppermute | solution.py:30
  312.5 98.0 %copy-start.2 = (s32[512]{0:T(512)S(1)}, s32[512]{0:T(512)}, u32[]{:S(2)}) copy-start(s32[512]{0:T(512)} %param.7) | copy-start | bytes 6148
  312.5 98.0 %copy-start.1 = (bf16[48,1024]{1,0:T(8,128)(2,1)S(1)}, bf16[48,1024]{1,0:T(8,128)(2,1)}, u32[]{:S(2)}) copy-start(bf16[48,1024]{1,0:T(8,128)(2,1)} %param.4) | copy-start | bytes 294916
  312.5 89.4 %collective-permute-start.1 = (f32[512,1024]{1,0:T(8,128)S(1)}, f32[512,1024]{1,0:T(8,128)S(1)}, u32[]{:S(2)}, u32[]{:S(2)}) collective-permute-start(f32[512,1024]{1,0:T(8,128)S(1)} %add.32), channel_id=1, source_target_pairs={{0,128},{64,192},{128,0},{192,64},{256,384},{320,448},{384,256},{4... | collective-permute-start | bytes 6291464 | tf_op jit(solution)/shard_map/ppermute | solution.py:30
  402.3 99.2 %collective-permute-start.2 = (f32[512,1024]{1,0:T(8,128)S(1)}, f32[512,1024]{1,0:T(8,128)}, u32[]{:S(2)}, u32[]{:S(2)}) collective-permute-start(f32[512,1024]{1,0:T(8,128)S(1)} %add.33), channel_id=1, source_target_pairs={{0,256},{64,320},{128,384},{192,448},{256,0},{320,64},{384,128},{4... | collective-permute-start | bytes 6291464 | tf_op jit(solution)/shard_map/ppermute | solution.py:30
  504.4 7.3 copy-start
Sparse Core Ops, SparseCore 0:
  11.3 88.3 all-gather.1
